TPU v7x, 32 devices: a whole 2x2x4 slice. The times are simulated.
32 devices in a mesh: groups: 2 (over y), pipe: 4 (over z), dp: 2 (over x), mp: 2 (over core).
Axes of the slice: x: 2, y: 2, z: 4, core: 2. Of those that a mesh axis runs over, the one named last changes fastest.
Arguments:
- latent: bfloat16 [4, 2, 2, 4, 16, 320], P(('groups', 'dp')), parts along dimension 0, may hold values from -6 to 6
- section_weight: bfloat16 [4, 2, 921600], P('pipe', None, 'mp'), may hold values from -0.01613743 to 0.01613743, as said below
- out_grad: bfloat16 [4, 2, 2, 4, 16, 320], P(('groups', 'dp')), parts along dimension 0, may hold values from -0.29882812 to 0.29882812
Outputs:
- section_grad: float32 [8, 921600], P(('groups', 'pipe'), 'mp'), parts along dimension 0
There are 2 independent parts, one for each index of `groups`. A program takes and returns all parts, laid end to end along the dimension named above; an argument that names none is the same for every part. Nothing has to cross between parts.
Inputs may be any that keep to these rules, and one draw needn't show every extreme that they name: section_weight[j, 0] equals section_weight[3 - j, 0] and section_weight[j, 1] equals section_weight[3 - j, 1] for every j: both devices of a mirrored pair hold the same two blocks.
All inputs are finite; a program needn't handle non-finite values.
Results may differ from a plain program's by a relative error of at most 0.0065.
Values may be sent and summed in bfloat16 or wider, within the bound.
No kernel may reach another device: no remote copies, remote signals or barrier semaphores. Data moves between devices by JAX's collectives and lax.ppermute only.
A program may use at most 64 MiB of HBM per device.

v0:
```python
import jax
import jax.numpy as jnp
from jax import lax
from jax.sharding import PartitionSpec as P


def shifted_2(block, axis, distance):
    devices = range(lax.axis_size(axis))
    route = [(i - distance, i) for i in devices if i - distance in devices]
    return lax.ppermute(block, axis, route)


def patches(image_in):
    img_rows, img_cols, channels = (image_in.shape[-3], image_in.shape[-2], image_in.shape[-1])
    padded = jnp.pad(image_in, [(0, 0)] * (image_in.ndim - 3) + [(1, 1), (1, 1), (0, 0)])
    shifted = [
        padded[..., row_off : row_off + img_rows, col_off : col_off + img_cols, :]
        for row_off in range(3)
        for col_off in range(3)
    ]
    return jnp.stack(shifted, axis=-2).reshape(-1, 9 * channels)


def silu_slope(pre_act):
    sigmoid = jax.nn.sigmoid(pre_act)
    return sigmoid * (1.0 + pre_act * (1.0 - sigmoid))


def mirror(payload):
    blocks = payload.reshape(lax.axis_size("pipe"), -1)
    spread = lax.all_to_all(blocks, "pipe", split_axis=0, concat_axis=0, tiled=True)
    returned = lax.all_to_all(jnp.flip(spread, 0), "pipe", split_axis=0, concat_axis=0, tiled=True)
    return returned.reshape(payload.shape)


def mirror_sums(payload):
    blocks = payload.reshape(lax.axis_size("pipe"), -1)
    spread = lax.all_to_all(blocks, "pipe", split_axis=0, concat_axis=0, tiled=True)
    returned = lax.all_to_all(jnp.flip(spread, 0), "pipe", split_axis=0, concat_axis=0, tiled=True)
    return returned.reshape(payload.shape)


def pass_on(payload, from_below):
    from_lower = shifted_2(payload, "pipe", 1)
    from_upper = shifted_2(payload, "pipe", -1)
    return (
        jnp.where(from_below, from_lower, from_upper),
        jnp.where(from_below, from_upper, from_lower),
    )


def take_slot(buffer, slot_index):
    return lax.dynamic_index_in_dim(buffer, slot_index, 0, keepdims=False)


def put_slot(buffer, payload, slot_index, active):
    return jnp.where(
        active, lax.dynamic_update_index_in_dim(buffer, payload, slot_index, 0), buffer
    )


def run_forward(source, skip_in, weight_half, position, from_below, tick_count):
    micro_count = source.shape[0]
    img_rows, img_cols, channels = (source.shape[1], source.shape[2], source.shape[3])
    chan_half = weight_half.shape[0] // (9 * channels)
    offset = lax.axis_index("mp") * chan_half
    row_weight = weight_half.reshape(chan_half, 9 * channels)

    def one_tick(tick_idx, state_carry):
        incoming, inputs, actives, outputs, crossed = state_carry
        micro_idx = tick_idx - position
        active = (micro_idx >= 0) & (micro_idx < micro_count)
        clipped = jnp.clip(micro_idx, 0, micro_count - 1)
        current = jnp.where(position == 0, take_slot(source, clipped), incoming)
        pre_act = current.astype(jnp.float32) + take_slot(skip_in, clipped).astype(jnp.float32)
        activation = jax.nn.silu(pre_act).astype(jnp.bfloat16)
        conv_out = lax.dot_general(
            patches(activation),
            row_weight,
            (((1,), (1,)), ((), ())),
            preferred_element_type=jnp.float32,
        )
        own_part = lax.dynamic_slice_in_dim(current, offset, chan_half, 2)
        output_half = (
            own_part.astype(jnp.float32) + conv_out.reshape(img_rows, img_cols, chan_half)
        ).astype(jnp.bfloat16)
        output = lax.all_gather(output_half, "mp", axis=2, tiled=True)
        chosen, other_side = pass_on(output, from_below)
        return (
            chosen,
            put_slot(inputs, current, clipped, active),
            put_slot(actives, activation, clipped, active),
            put_slot(outputs, output, clipped, active),
            put_slot(crossed, other_side, clipped, active),
        )

    initial = (
        jnp.zeros_like(source[0]),
        jnp.zeros_like(source),
        jnp.zeros_like(source),
        jnp.zeros_like(source),
        jnp.zeros_like(source),
    )
    final_state = lax.fori_loop(0, tick_count, one_tick, initial)
    return (final_state[1], final_state[2], final_state[3], final_state[4])


def run_backward(
    extra_cot, inputs, actives, skip_in, weight_half, position, from_below, tick_count, end_flag
):
    micro_count = inputs.shape[0]
    img_rows, img_cols, channels = (inputs.shape[1], inputs.shape[2], inputs.shape[3])
    chan_half = weight_half.shape[0] // (9 * channels)
    offset = lax.axis_index("mp") * chan_half
    back_weight = (
        jnp.flip(weight_half.reshape(chan_half, 3, 3, channels), (1, 2))
        .transpose(1, 2, 0, 3)
        .reshape(9 * chan_half, channels)
    )

    def one_tick(tick_idx, state_carry):
        incoming, cot_parts, skip_terms = state_carry
        micro_idx = tick_idx - position
        active = (micro_idx >= 0) & (micro_idx < micro_count)
        clipped = jnp.clip(micro_idx, 0, micro_count - 1)
        received = jnp.where(position == 0, 0.0, incoming.astype(jnp.float32))
        cotangent = (received + take_slot(extra_cot, clipped)).astype(jnp.bfloat16)
        cot_half = lax.dynamic_slice_in_dim(cotangent, offset, chan_half, 2)
        partial_value = jnp.dot(
            patches(cot_half), back_weight, preferred_element_type=jnp.float32
        ).reshape(img_rows, img_cols, channels)
        summed = lax.psum(partial_value, "mp")
        pre_act = take_slot(inputs, clipped).astype(jnp.float32) + take_slot(
            skip_in, clipped
        ).astype(jnp.float32)
        slope_term = summed * silu_slope(pre_act)
        passed = (cotangent.astype(jnp.float32) + slope_term).astype(jnp.bfloat16)
        skip_term = (slope_term + jnp.where(end_flag, passed.astype(jnp.float32), 0.0)).astype(
            jnp.bfloat16
        )
        chosen, other_side = pass_on(passed, from_below)
        return (
            chosen,
            put_slot(cot_parts, cot_half, clipped, active),
            put_slot(skip_terms, skip_term, clipped, active),
        )

    initial = (
        jnp.zeros_like(inputs[0]),
        jnp.zeros((micro_count, img_rows, img_cols, chan_half), jnp.bfloat16),
        jnp.zeros_like(inputs),
    )
    final_state = lax.fori_loop(0, tick_count, one_tick, initial)
    weight_grad = lax.dot_general(
        final_state[1].reshape(-1, chan_half),
        patches(actives),
        (((0,), (0,)), ((), ())),
        preferred_element_type=jnp.float32,
    )
    return (weight_grad.reshape(weight_half.shape), final_state[2])


def local(latent, section_weight, out_grad):
    pipe_size = lax.axis_size("pipe")
    half_size = pipe_size // 2
    device = lax.axis_index("pipe")
    lower_half = device < half_size
    upper_half = jnp.logical_not(lower_half)
    pair_index = jnp.minimum(device, pipe_size - 1 - device)
    tick_count = half_size + latent.shape[2] - 1
    encoder_weight = section_weight[0, 0]
    decoder_weight = section_weight[0, 1]
    first_dir = jnp.where(lower_half, 0, 1)
    samples = take_slot(latent[0], first_dir)
    zero_skip = jnp.zeros_like(samples)
    enc_inputs, enc_acts, enc_out, middle_in = run_forward(
        samples, zero_skip, encoder_weight, pair_index, lower_half, tick_count
    )
    skip_in = mirror(enc_out)
    dec_source = jnp.where(pair_index == half_size - 1, middle_in, skip_in)
    dec_inputs, dec_acts, dec_out, unused_in = run_forward(
        dec_source, skip_in, decoder_weight, half_size - 1 - pair_index, upper_half, tick_count
    )
    seed_cot = take_slot(out_grad[0], 1 - first_dir).astype(jnp.float32)
    seed_cot = jnp.where(pair_index == 0, seed_cot, 0.0)
    decoder_grad, dec_terms = run_backward(
        seed_cot,
        dec_inputs,
        dec_acts,
        skip_in,
        decoder_weight,
        pair_index,
        lower_half,
        tick_count,
        pair_index == half_size - 1,
    )
    terms_in = mirror(dec_terms).astype(jnp.float32)
    encoder_grad, enc_terms = run_backward(
        terms_in,
        enc_inputs,
        enc_acts,
        zero_skip,
        encoder_weight,
        half_size - 1 - pair_index,
        upper_half,
        tick_count,
        False,
    )
    kept_grad = jnp.where(lower_half, encoder_grad, decoder_grad)
    sent_grad = jnp.where(lower_half, decoder_grad, encoder_grad)
    combined = kept_grad + mirror_sums(sent_grad)
    combined = lax.psum(combined, "dp")
    return combined.reshape(1, -1)


def solution(mesh):
    return jax.shard_map(
        local,
        mesh=mesh,
        in_specs=(
            P(("groups", "dp"), None, None, None, None, None),
            P("pipe", None, "mp"),
            P(("groups", "dp"), None, None, None, None, None),
        ),
        out_specs=P(("groups", "pipe"), "mp"),
        check_vma=False,
    )
```

profile of v0, /device:TPU:0, one launch (start us, length us, event | category | flops | bytes accessed | tf_op | source)
XLA Modules:
  0.0 979.8 jit_solution(13960116564052826964)
XLA Ops:
  7.4 21.7 %slice_reduce_fusion = (bf16[460800]{0:T(1024)(128)(2,1)S(1)}, bf16[460800]{0:T(1024)(128)(2,1)}) fusion(bf16[1,2,460800]{2,1,0:T(2,128)(2,1)} %param.12), kind=kLoop, calls=%fused_computation.170 | loop fusion | bytes 3686400 | tf_op jit(solution)/shard_map/slice | solution.py:171
  31.8 46.2 %while.82 = (s32[]{:T(128)}, bf16[4,16,320]{2,1,0:T(8,128)(2,1)S(1)}, bf16[2,4,16,320]{3,2,1,0:T(8,128)(2,1)S(1)}, bf16[2,4,16,320]{3,2,1,0:T(8,128)(2,1)S(1)}, ...) while((s32[]{:T(128)}, ...), condition=%wide.region_1.2_spmd.clone, body=%wide.region_0.1_spmd.clone.sunk | while | flops 59545608 | bytes 6439339 | solution.py:104
  36.7 4.8 collective-permute-start
  85.1 5.5 all-to-all-done
  108.3 8.3 rev.18
  118.0 11.2 %rev.21 = bf16[160,3,3,320]{3,2,1,0:T(4,128)(2,1)} reverse(bf16[160,3,3,320]{3,2,1,0:T(4,128)(2,1)} %reshape_squeeze.15), dimensions={1,2} | reverse | bytes 1843200 | tf_op jit(solution)/shard_map/jit(_flip)/rev | solution.py:116
  135.4 69.2 %while.83 = (s32[]{:T(128)}, bf16[4,16,320]{1,0,2:T(4,128)(2,1)}, bf16[2,4,16,320]{3,2,1,0:T(8,128)(2,1)}, bf16[2,4,16,320]{3,2,1,0:T(8,128)(2,1)S(1)}, pred[]{:...) while((s32[]{:T(128)}, bf16[4,16,320]{1,0,2:T(4,128)(2,1)}, ...), condition=%wide.region_3.4_spmd.clone, body=%wide.region_2.3_spmd.clone.sunk | while | flops 59279368 | bytes 5611900 | solution.py:104
  148.0 5.9 collective-permute-done.2
  170.9 5.9 collective-permute-done.2
  193.8 5.9 collective-permute-done.2
  205.7 95.1 %while.84 = (s32[]{:T(128)}, bf16[4,16,320]{2,1,0:T(8,128)(2,1)}, bf16[2,4,16,160]{3,2,1,0:T(8,128)(2,1)S(1)}, bf16[2,4,16,320]{3,2,1,0:T(8,128)(2,1)S(1)}, pred...) while((s32[]{:T(128)}, bf16[4,16,320]{2,1,0:T(8,128)(2,1)}, ...), condition=%wide.region_6.7_spmd.clone, body=%wide.region_4.6_spmd.clone.sunk | while | flops 59811848 | bytes 4673925 | solution.py:153
  208.8 16.3 %all-reduce.12.cloned.1.call-done = f32[4,16,320]{2,1,0:T(8,128)} async-done(((f32[4,16,320]{2,1,0:T(8,128)}), f32[4,16,320]{2,1,0:T(8,128)}) %all-reduce.12.cloned.1.call-update) | async-done | bytes 81936 | tf_op jit(solution)/shard_map/while/body/eval_jaxpr/psum | solution.py:132
  239.2 18.1 %all-reduce.12.cloned.1.call-done = f32[4,16,320]{2,1,0:T(8,128)} async-done(((f32[4,16,320]{2,1,0:T(8,128)}), f32[4,16,320]{2,1,0:T(8,128)}) %all-reduce.12.cloned.1.call-update) | async-done | bytes 81936 | tf_op jit(solution)/shard_map/while/body/eval_jaxpr/psum | solution.py:132
  271.5 18.1 %all-reduce.12.cloned.1.call-done = f32[4,16,320]{2,1,0:T(8,128)} async-done(((f32[4,16,320]{2,1,0:T(8,128)}), f32[4,16,320]{2,1,0:T(8,128)}) %all-reduce.12.cloned.1.call-update) | async-done | bytes 81936 | tf_op jit(solution)/shard_map/while/body/eval_jaxpr/psum | solution.py:132
  325.6 94.5 %while.85 = (s32[]{:T(128)}, bf16[4,16,320]{2,1,0:T(8,128)(2,1)S(1)}, bf16[2,4,16,160]{3,2,1,0:T(8,128)(2,1)S(1)}, pred[]{:T(512)}, pred[]{:T(512)}, /*index=5*/...) while((s32[]{:T(128)}, ...), condition=%wide.region_9.10_spmd.clone, body=%wide.region_7.9_spmd.clone.sunk | while | flops 59381768 | bytes 3977547 | solution.py:153
  327.7 19.0 %all-reduce.14.cloned.1.call-done = f32[4,16,320]{2,1,0:T(8,128)} async-done(((f32[4,16,320]{2,1,0:T(8,128)}), f32[4,16,320]{2,1,0:T(8,128)}) %all-reduce.14.cloned.1.call-update) | async-done | bytes 81936 | tf_op jit(solution)/shard_map/while/body/eval_jaxpr/psum | solution.py:132
  359.5 18.7 %all-reduce.14.cloned.1.call-done = f32[4,16,320]{2,1,0:T(8,128)} async-done(((f32[4,16,320]{2,1,0:T(8,128)}), f32[4,16,320]{2,1,0:T(8,128)}) %all-reduce.14.cloned.1.call-update) | async-done | bytes 81936 | tf_op jit(solution)/shard_map/while/body/eval_jaxpr/psum | solution.py:132
  390.8 18.7 %all-reduce.14.cloned.1.call-done = f32[4,16,320]{2,1,0:T(8,128)} async-done(((f32[4,16,320]{2,1,0:T(8,128)}), f32[4,16,320]{2,1,0:T(8,128)}) %all-reduce.14.cloned.1.call-update) | async-done | bytes 81936 | tf_op jit(solution)/shard_map/while/body/eval_jaxpr/psum | solution.py:132
  422.9 4.7 select_n.488
  427.7 45.6 %all_to_all.62 = f32[4,1,115200]{2,1,0:T(1,128)S(1)} all-to-all(f32[4,1,115200]{2,1,0:T(1,128)} %select_n.488), channel_id=1, replica_groups=mesh['groups'=2,'pipe'=4,'dp'=2,'mp'=2] {'pipe'}, dimensions={0} | all-to-all | bytes 3686400 | tf_op jit(solution)/shard_map/all_to_all | solution.py:38
  475.0 383.0 %rev.22 = f32[4,115200]{1,0:T(4,128)} reverse(f32[4,115200]{1,0:T(4,128)} %bitcast.459), dimensions={0} | reverse | bytes 3686400 | tf_op jit(solution)/shard_map/jit(_flip)/rev | solution.py:39
  858.0 4.7 copy.61
  869.4 39.5 %all-to-all-done.5 = f32[4,1,115200]{2,1,0:T(1,128)} async-done(((f32[4,1,115200]{2,1,0:T(1,128)}), f32[4,1,115200]{2,1,0:T(1,128)}, u32[]{:S(2)}, u32[]{:S(2)}) %all-to-all-start.5) | async-done | bytes 1843232 | tf_op jit(solution)/shard_map/all_to_all | solution.py:39
  912.3 56.3 %all-reduce.10.cloned.1.call-done = f32[1,460800]{1,0:T(1,128)} async-done(((f32[1,460800]{1,0:T(1,128)}), f32[1,460800]{1,0:T(1,128)}) %all-reduce.10.cloned.1.call-update) | async-done | bytes 1843216 | tf_op jit(solution)/shard_map/psum | solution.py:212
  (427 shorter events, 251.1 us)
Async XLA Ops:
  36.7 6.6 collective-permute-start
  41.5 6.0 collective-permute-start.1
  56.4 6.0 collective-permute-start.1
  71.4 6.0 collective-permute-start.1
  81.5 9.1 all-to-all-start
  94.2 39.2 %all-to-all-start.1 = ((bf16[4,2,5120]{2,1,0:T(2,128)(2,1)}), bf16[4,2,5120]{2,1,0:T(2,128)(2,1)S(1)}, u32[]{:S(2)}, u32[]{:S(2)}) async-start(bf16[4,2,5120]{2,1,0:T(2,128)(2,1)} %reshape.168), calls=%async_computation.1 | async-start | bytes 163840 | tf_op jit(solution)/shard_map/all_to_all | solution.py:32
  142.9 11.0 %collective-permute-start.2 = (bf16[4,16,320]{1,0,2:T(4,128)(2,1)S(1)}, bf16[4,16,320]{1,0,2:T(4,128)(2,1)S(1)}, u32[]{:S(2)}, u32[]{:S(2)}) collective-permute-start(bf16[4,16,320]{1,0,2:T(4,128)(2,1)S(1)} %all_gather.25), channel_id=1, source_target_pairs={{0,4},{4,8},{8,12},{1,5},{5,9},{9,13},{2,6},{6,10},{10,14},{3,7},{... | collective-permute-start | bytes 122888 | tf_op jit(solution)/shard_map/while/body/eval_jaxpr/ppermute | solution.py:10
  146.6 11.4 %collective-permute-start.3 = (bf16[4,16,320]{1,0,2:T(4,128)(2,1)S(1)}, bf16[4,16,320]{1,0,2:T(4,128)(2,1)S(1)}, u32[]{:S(2)}, u32[]{:S(2)}) collective-permute-start(bf16[4,16,320]{1,0,2:T(4,128)(2,1)S(1)} %all_gather.25), channel_id=1, source_target_pairs={{4,0},{8,4},{12,8},{5,1},{9,5},{13,9},{6,2},{10,6},{14,10},{7,3},{... | collective-permute-start | bytes 122888 | tf_op jit(solution)/shard_map/while/body/eval_jaxpr/ppermute | solution.py:10
  166.2 10.6 %collective-permute-start.2 = (bf16[4,16,320]{1,0,2:T(4,128)(2,1)S(1)}, bf16[4,16,320]{1,0,2:T(4,128)(2,1)S(1)}, u32[]{:S(2)}, u32[]{:S(2)}) collective-permute-start(bf16[4,16,320]{1,0,2:T(4,128)(2,1)S(1)} %all_gather.25), channel_id=1, source_target_pairs={{0,4},{4,8},{8,12},{1,5},{5,9},{9,13},{2,6},{6,10},{10,14},{3,7},{... | collective-permute-start | bytes 122888 | tf_op jit(solution)/shard_map/while/body/eval_jaxpr/ppermute | solution.py:10
  169.5 11.4 %collective-permute-start.3 = (bf16[4,16,320]{1,0,2:T(4,128)(2,1)S(1)}, bf16[4,16,320]{1,0,2:T(4,128)(2,1)S(1)}, u32[]{:S(2)}, u32[]{:S(2)}) collective-permute-start(bf16[4,16,320]{1,0,2:T(4,128)(2,1)S(1)} %all_gather.25), channel_id=1, source_target_pairs={{4,0},{8,4},{12,8},{5,1},{9,5},{13,9},{6,2},{10,6},{14,10},{7,3},{... | collective-permute-start | bytes 122888 | tf_op jit(solution)/shard_map/while/body/eval_jaxpr/ppermute | solution.py:10
  189.1 10.6 %collective-permute-start.2 = (bf16[4,16,320]{1,0,2:T(4,128)(2,1)S(1)}, bf16[4,16,320]{1,0,2:T(4,128)(2,1)S(1)}, u32[]{:S(2)}, u32[]{:S(2)}) collective-permute-start(bf16[4,16,320]{1,0,2:T(4,128)(2,1)S(1)} %all_gather.25), channel_id=1, source_target_pairs={{0,4},{4,8},{8,12},{1,5},{5,9},{9,13},{2,6},{6,10},{10,14},{3,7},{... | collective-permute-start | bytes 122888 | tf_op jit(solution)/shard_map/while/body/eval_jaxpr/ppermute | solution.py:10
  192.5 11.4 %collective-permute-start.3 = (bf16[4,16,320]{1,0,2:T(4,128)(2,1)S(1)}, bf16[4,16,320]{1,0,2:T(4,128)(2,1)S(1)}, u32[]{:S(2)}, u32[]{:S(2)}) collective-permute-start(bf16[4,16,320]{1,0,2:T(4,128)(2,1)S(1)} %all_gather.25), channel_id=1, source_target_pairs={{4,0},{8,4},{12,8},{5,1},{9,5},{13,9},{6,2},{10,6},{14,10},{7,3},{... | collective-permute-start | bytes 122888 | tf_op jit(solution)/shard_map/while/body/eval_jaxpr/ppermute | solution.py:10
  205.7 19.3 %all-reduce.12.cloned.1.call-start = ((), (), s32[]{:S(2)}) async-start(), calls=%async_computation.7 | async-start | bytes 196608 | tf_op jit(solution)/shard_map/while/body/eval_jaxpr/psum | solution.py:132
  229.6 6.0 collective-permute-start.5
  236.2 21.1 %all-reduce.12.cloned.1.call-start = ((), (), s32[]{:S(2)}) async-start(), calls=%async_computation.7 | async-start | bytes 196608 | tf_op jit(solution)/shard_map/while/body/eval_jaxpr/psum | solution.py:132
  261.9 6.0 collective-permute-start.5
  268.5 21.1 %all-reduce.12.cloned.1.call-start = ((), (), s32[]{:S(2)}) async-start(), calls=%async_computation.7 | async-start | bytes 196608 | tf_op jit(solution)/shard_map/while/body/eval_jaxpr/psum | solution.py:132
  302.8 9.5 all-to-all-start.2
  315.8 9.1 all-to-all-start.3
  325.6 21.1 %all-reduce.14.cloned.1.call-start = ((), (), s32[]{:S(2)}) async-start(), calls=%async_computation.8 | async-start | bytes 196608 | tf_op jit(solution)/shard_map/while/body/eval_jaxpr/psum | solution.py:132
  357.4 20.8 %all-reduce.14.cloned.1.call-start = ((), (), s32[]{:S(2)}) async-start(), calls=%async_computation.8 | async-start | bytes 196608 | tf_op jit(solution)/shard_map/while/body/eval_jaxpr/psum | solution.py:132
  388.7 20.8 %all-reduce.14.cloned.1.call-start = ((), (), s32[]{:S(2)}) async-start(), calls=%async_computation.8 | async-start | bytes 196608 | tf_op jit(solution)/shard_map/while/body/eval_jaxpr/psum | solution.py:132
  862.7 46.2 %all-to-all-start.5 = ((f32[4,1,115200]{2,1,0:T(1,128)}), f32[4,1,115200]{2,1,0:T(1,128)}, u32[]{:S(2)}, u32[]{:S(2)}) async-start(f32[4,1,115200]{2,1,0:T(1,128)} %copy.61), calls=%async_computation.5 | async-start | bytes 3686400 | tf_op jit(solution)/shard_map/all_to_all | solution.py:39
  867.1 101.6 %all-reduce.10.cloned.1.call-start = ((), (), s32[]{:S(2)}) async-start(), calls=%async_computation.6 | async-start | bytes 3686400 | tf_op jit(solution)/shard_map/psum | solution.py:212
  (47 other events, 466.7 us)
Sparse Core Ops, SparseCore 0:
  209.0 16.0 all-reduce.11
  239.5 17.7 all-reduce.11
  271.7 17.7 all-reduce.11
  328.5 18.1 all-reduce.13
  360.3 17.7 all-reduce.13
  391.7 17.7 all-reduce.13
Sparse Core Ops, SparseCore 1:
  912.4 56.2 all-reduce.9
where the time goes:
time: 997 us; the launch traced here: 980 us
  local copies, waits for them, and re-layouts  493 us (49%)
  waiting for transfers between devices  284 us (28%)
  starting transfers between devices  78.3 us (8%)
  blocking collectives  58 us (6%)
  other arithmetic  34.1 us (3%)
  between operations  15.3 us (2%)
  matrix products  14.9 us (1%)
    rev x1, local copies, waits for them, and re-layouts, mirror_sums(): jnp.flip(spread, 0)  383 us
    psum x6, waiting for transfers between devices, one_tick(): summed = lax.psum(partial_value, 'mp')  109 us
    ppermute x24, waiting for transfers between devices, shifted_2(): return lax.ppermute(block, axis, route)  69 us
    ppermute x24, starting transfers between devices, shifted_2(): return lax.ppermute(block, axis, route)  59.7 us
    psum x1, waiting for transfers between devices, local(): combined = lax.psum(combined, 'dp')  56.3 us
    all_to_all x1, blocking collectives, mirror_sums(): lax.all_to_all(blocks, 'pipe', split_axis=0, concat_axis=0, tiled=True)  45.6 us
    all_to_all x1, waiting for transfers between devices, mirror_sums(): lax.all_to_all(jnp.flip(spread, 0), 'pipe', split_axis=0, concat_axis=0,...  39.5 us
    slice x1, local copies, waits for them, and re-layouts, local(): encoder_weight = section_weight[0, 0]  21.7 us
  transfers between devices with their start and end apart: 36, of which 32 were waited for; matrix products, arithmetic and copies ran while one was open for 5% of the time, Pallas kernels for 0%

commit v1 on v0

--- a/solution.py
+++ b/solution.py
@@ -1,7 +1,45 @@
+import functools
 import jax
 import jax.numpy as jnp
 from jax import lax
 from jax.sharding import PartitionSpec as P
+
+
+def _assign_threads(local_values, axis_no, original):
+    piece_now, tile_out = (local_values.shape[:axis_no], local_values.shape[axis_no + 1 :])
+    arr_next = jnp.moveaxis(local_values.reshape(*piece_now, original, -1, *tile_out), axis_no, 0)
+    return arr_next
+
+
+def remake_tiles_by_axis(v0, axis_k):
+    v0 = jnp.moveaxis(v0, 0, axis_k)
+    back = v0.shape
+    answer = v0.reshape(*back[:axis_k], back[axis_k] * back[axis_k + 1], *back[axis_k + 2 :])
+    return answer
+
+
+def _prepare_words(slab_in, along_axis, inp, buf):
+    carry_out = jax.lax.psum(1, along_axis)
+    z2 = jax.lax.axis_index(along_axis)
+    w1, v1 = (carry_out, z2)
+    x_now = _assign_threads(slab_in, inp, w1)
+    gallery = [x_now[v1]]
+    q = 1
+    while q < w1:
+        side_arr = x_now[v1 ^ q]
+        gallery.append(
+            jax.lax.ppermute(
+                side_arr, axis_name=along_axis, perm=[(k0, k0 ^ q) for k0 in range(w1)]
+            )
+        )
+        q += 1
+    step_out = jnp.stack(gallery, axis=0)
+    x_now = step_out[v1 ^ jnp.arange(w1)]
+    next_value = remake_tiles_by_axis(x_now, buf)
+    return next_value
+
+
+_cut_panel = functools.partial(_prepare_words, along_axis="pipe", inp=0, buf=0)
 
 
 def shifted_2(block, axis, distance):
@@ -35,7 +73,7 @@
 
 def mirror_sums(payload):
     blocks = payload.reshape(lax.axis_size("pipe"), -1)
-    spread = lax.all_to_all(blocks, "pipe", split_axis=0, concat_axis=0, tiled=True)
+    spread = _cut_panel(blocks)
     returned = lax.all_to_all(jnp.flip(spread, 0), "pipe", split_axis=0, concat_axis=0, tiled=True)
     return returned.reshape(payload.shape)
 

time: 997 us -> 927 us (0.930)
  local copies, waits for them, and re-layouts: 493 us -> 428 us
  blocking collectives: 58 us -> 12.3 us
  waiting for transfers between devices: 284 us -> 315 us
  starting transfers between devices: 78.3 us -> 88.6 us
    rev x1 -> x0, local copies, waits for them, and re-layouts: 383 us -> none  [mirror_sums(): jnp.flip(spread, 0)]
    unnamed x52 -> x54, local copies, waits for them, and re-layouts: 14.8 us -> 329 us
    all_to_all x1 -> x0, blocking collectives: 45.6 us -> none  [mirror_sums(): lax.all_to_all(blocks, 'pipe', split_axis=0, concat_axis=0, tiled=True)]
    ppermute x0 -> x3, waiting for transfers between devices: none -> 31.2 us  [_prepare_words(): jax.lax.ppermute(side_arr, axis_name=along_axis, perm=[(k0, k0 ^ q) for k...]
  transfers between devices with their start and end apart: 36 -> 39, of which waited for: 32 -> 34; matrix products, arithmetic and copies ran while one was open for 5% -> 5% of each run, Pallas kernels for 0% -> 0%
where the time goes in v1:
time: 927 us; the launch traced here: 912 us
  local copies, waits for them, and re-layouts  428 us (46%)
  waiting for transfers between devices  315 us (34%)
  starting transfers between devices  88.6 us (10%)
  other arithmetic  36.2 us (4%)
  between operations  15.3 us (2%)
  matrix products  14.9 us (2%)
  blocking collectives  12.3 us (1%)
    unnamed x54, local copies, waits for them, and re-layouts  329 us
    psum x6, waiting for transfers between devices, one_tick(): summed = lax.psum(partial_value, 'mp')  109 us
    ppermute x24, waiting for transfers between devices, shifted_2(): return lax.ppermute(block, axis, route)  69 us
    ppermute x24, starting transfers between devices, shifted_2(): return lax.ppermute(block, axis, route)  59.7 us
    psum x1, waiting for transfers between devices, local(): combined = lax.psum(combined, 'dp')  56.3 us
    all_to_all x1, waiting for transfers between devices, mirror_sums(): lax.all_to_all(jnp.flip(spread, 0), 'pipe', split_axis=0, concat_axis=0,...  39.2 us
    ppermute x3, waiting for transfers between devices, _prepare_words(): jax.lax.ppermute(side_arr, axis_name=along_axis, perm=[(k0, k0 ^ q) for k...  31.2 us
    slice x1, local copies, waits for them, and re-layouts, local(): encoder_weight = section_weight[0, 0]  21.7 us
  transfers between devices with their start and end apart: 39, of which 34 were waited for; matrix products, arithmetic and copies ran while one was open for 5% of the time, Pallas kernels for 0%

profile of v1, /device:TPU:0, one launch (start us, length us, event | category | flops | bytes accessed | tf_op | source)
XLA Modules:
  0.0 912.2 jit_solution(10739663174352963998)
XLA Ops:
  7.4 21.7 %slice_reduce_fusion = (bf16[460800]{0:T(1024)(128)(2,1)S(1)}, bf16[460800]{0:T(1024)(128)(2,1)}) fusion(bf16[1,2,460800]{2,1,0:T(2,128)(2,1)} %param.12), kind=kLoop, calls=%fused_computation.171 | loop fusion | bytes 3686400 | tf_op jit(solution)/shard_map/slice | solution.py:209
  31.9 46.3 %while.82 = (s32[]{:T(128)}, bf16[4,16,320]{2,1,0:T(8,128)(2,1)S(1)}, bf16[2,4,16,320]{3,2,1,0:T(8,128)(2,1)S(1)}, bf16[2,4,16,320]{3,2,1,0:T(8,128)(2,1)S(1)}, ...) while((s32[]{:T(128)}, ...), condition=%wide.region_1.2_spmd.clone, body=%wide.region_0.1_spmd.clone.sunk | while | flops 59545608 | bytes 6439339 | solution.py:142
  85.3 5.5 all-to-all-done
  108.6 8.3 rev.18
  118.2 11.2 %rev.21 = bf16[160,3,3,320]{3,2,1,0:T(4,128)(2,1)} reverse(bf16[160,3,3,320]{3,2,1,0:T(4,128)(2,1)} %reshape_squeeze.15), dimensions={1,2} | reverse | bytes 1843200 | tf_op jit(solution)/shard_map/jit(_flip)/rev | solution.py:154
  135.7 69.3 %while.83 = (s32[]{:T(128)}, bf16[4,16,320]{1,0,2:T(4,128)(2,1)}, bf16[2,4,16,320]{3,2,1,0:T(8,128)(2,1)}, bf16[2,4,16,320]{3,2,1,0:T(8,128)(2,1)S(1)}, pred[]{:...) while((s32[]{:T(128)}, bf16[4,16,320]{1,0,2:T(4,128)(2,1)}, ...), condition=%wide.region_3.4_spmd.clone, body=%wide.region_2.3_spmd.clone.sunk | while | flops 59279368 | bytes 5611900 | solution.py:142
  148.2 5.9 collective-permute-done.2
  171.2 5.9 collective-permute-done.2
  194.2 5.9 collective-permute-done.2
  206.1 95.1 %while.84 = (s32[]{:T(128)}, bf16[4,16,320]{2,1,0:T(8,128)(2,1)}, bf16[2,4,16,160]{3,2,1,0:T(8,128)(2,1)S(1)}, bf16[2,4,16,320]{3,2,1,0:T(8,128)(2,1)S(1)}, pred...) while((s32[]{:T(128)}, bf16[4,16,320]{2,1,0:T(8,128)(2,1)}, ...), condition=%wide.region_6.7_spmd.clone, body=%wide.region_4.6_spmd.clone.sunk | while | flops 59811848 | bytes 4673925 | solution.py:191
  209.1 16.3 %all-reduce.12.cloned.1.call-done = f32[4,16,320]{2,1,0:T(8,128)} async-done(((f32[4,16,320]{2,1,0:T(8,128)}), f32[4,16,320]{2,1,0:T(8,128)}) %all-reduce.12.cloned.1.call-update) | async-done | bytes 81936 | tf_op jit(solution)/shard_map/while/body/eval_jaxpr/psum | solution.py:170
  239.6 18.1 %all-reduce.12.cloned.1.call-done = f32[4,16,320]{2,1,0:T(8,128)} async-done(((f32[4,16,320]{2,1,0:T(8,128)}), f32[4,16,320]{2,1,0:T(8,128)}) %all-reduce.12.cloned.1.call-update) | async-done | bytes 81936 | tf_op jit(solution)/shard_map/while/body/eval_jaxpr/psum | solution.py:170
  271.9 18.1 %all-reduce.12.cloned.1.call-done = f32[4,16,320]{2,1,0:T(8,128)} async-done(((f32[4,16,320]{2,1,0:T(8,128)}), f32[4,16,320]{2,1,0:T(8,128)}) %all-reduce.12.cloned.1.call-update) | async-done | bytes 81936 | tf_op jit(solution)/shard_map/while/body/eval_jaxpr/psum | solution.py:170
  326.1 94.5 %while.85 = (s32[]{:T(128)}, bf16[4,16,320]{2,1,0:T(8,128)(2,1)S(1)}, bf16[2,4,16,160]{3,2,1,0:T(8,128)(2,1)S(1)}, pred[]{:T(512)}, pred[]{:T(512)}, /*index=5*/...) while((s32[]{:T(128)}, ...), condition=%wide.region_9.10_spmd.clone, body=%wide.region_7.9_spmd.clone.sunk | while | flops 59381768 | bytes 3977547 | solution.py:191
  328.2 19.0 %all-reduce.14.cloned.1.call-done = f32[4,16,320]{2,1,0:T(8,128)} async-done(((f32[4,16,320]{2,1,0:T(8,128)}), f32[4,16,320]{2,1,0:T(8,128)}) %all-reduce.14.cloned.1.call-update) | async-done | bytes 81936 | tf_op jit(solution)/shard_map/while/body/eval_jaxpr/psum | solution.py:170
  359.9 18.6 %all-reduce.14.cloned.1.call-done = f32[4,16,320]{2,1,0:T(8,128)} async-done(((f32[4,16,320]{2,1,0:T(8,128)}), f32[4,16,320]{2,1,0:T(8,128)}) %all-reduce.14.cloned.1.call-update) | async-done | bytes 81936 | tf_op jit(solution)/shard_map/while/body/eval_jaxpr/psum | solution.py:170
  391.3 18.6 %all-reduce.14.cloned.1.call-done = f32[4,16,320]{2,1,0:T(8,128)} async-done(((f32[4,16,320]{2,1,0:T(8,128)}), f32[4,16,320]{2,1,0:T(8,128)}) %all-reduce.14.cloned.1.call-update) | async-done | bytes 81936 | tf_op jit(solution)/shard_map/while/body/eval_jaxpr/psum | solution.py:170
  425.7 5.1 constant_dynamic-slice_fusion.2
  435.3 15.5 %collective-permute-done.8 = f32[1,115200]{1,0:T(1,128)S(1)} collective-permute-done((f32[1,115200]{1,0:T(1,128)S(1)}, f32[1,115200]{1,0:T(1,128)S(1)}, u32[]{:S(2)}, u32[]{:S(2)}) %collective-permute-start.8) | collective-permute-done | bytes 460832 | tf_op jit(solution)/shard_map/ppermute | solution.py:31
  450.8 15.7 %collective-permute-done.9 = f32[1,115200]{1,0:T(1,128)S(1)} collective-permute-done((f32[1,115200]{1,0:T(1,128)S(1)}, f32[1,115200]{1,0:T(1,128)S(1)}, u32[]{:S(2)}, u32[]{:S(2)}) %collective-permute-start.9) | collective-permute-done | bytes 460832 | tf_op jit(solution)/shard_map/ppermute | solution.py:31
  470.8 315.5 %reverse = f32[4,115200]{1,0:T(4,128)S(1)} reverse(f32[4,115200]{1,0:T(4,128)} %gather_fusion), dimensions={0} | reverse | bytes 3686400
  789.5 10.4 %all-to-all-start.4 = ((f32[4,1,115200]{2,1,0:T(1,128)}), f32[4,1,115200]{2,1,0:T(1,128)}, u32[]{:S(2)}, u32[]{:S(2)}) async-start(f32[4,1,115200]{2,1,0:T(1,128)} %copy.59), calls=%async_computation.4 | async-start | bytes 3686400 | tf_op jit(solution)/shard_map/all_to_all | solution.py:77
  802.1 39.2 %all-to-all-done.4 = f32[4,1,115200]{2,1,0:T(1,128)} async-done(((f32[4,1,115200]{2,1,0:T(1,128)}), f32[4,1,115200]{2,1,0:T(1,128)}, u32[]{:S(2)}, u32[]{:S(2)}) %all-to-all-start.4) | async-done | bytes 1843232 | tf_op jit(solution)/shard_map/all_to_all | solution.py:77
  844.8 56.3 %all-reduce.10.cloned.1.call-done = f32[1,460800]{1,0:T(1,128)} async-done(((f32[1,460800]{1,0:T(1,128)}), f32[1,460800]{1,0:T(1,128)}) %all-reduce.10.cloned.1.call-update) | async-done | bytes 1843216 | tf_op jit(solution)/shard_map/psum | solution.py:250
  (438 shorter events, 264.4 us)
Async XLA Ops:
  36.7 6.6 collective-permute-start
  71.5 6.0 collective-permute-start.1
  81.7 9.1 all-to-all-start
  94.4 39.3 %all-to-all-start.1 = ((bf16[4,2,5120]{2,1,0:T(2,128)(2,1)}), bf16[4,2,5120]{2,1,0:T(2,128)(2,1)S(1)}, u32[]{:S(2)}, u32[]{:S(2)}) async-start(bf16[4,2,5120]{2,1,0:T(2,128)(2,1)} %reshape.196), calls=%async_computation.1 | async-start | bytes 163840 | tf_op jit(solution)/shard_map/all_to_all | solution.py:70
  143.2 11.0 %collective-permute-start.2 = (bf16[4,16,320]{1,0,2:T(4,128)(2,1)S(1)}, bf16[4,16,320]{1,0,2:T(4,128)(2,1)S(1)}, u32[]{:S(2)}, u32[]{:S(2)}) collective-permute-start(bf16[4,16,320]{1,0,2:T(4,128)(2,1)S(1)} %all_gather.25), channel_id=1, source_target_pairs={{0,4},{4,8},{8,12},{1,5},{5,9},{9,13},{2,6},{6,10},{10,14},{3,7},{... | collective-permute-start | bytes 122888 | tf_op jit(solution)/shard_map/while/body/eval_jaxpr/ppermute | solution.py:48
  146.9 11.4 %collective-permute-start.3 = (bf16[4,16,320]{1,0,2:T(4,128)(2,1)S(1)}, bf16[4,16,320]{1,0,2:T(4,128)(2,1)S(1)}, u32[]{:S(2)}, u32[]{:S(2)}) collective-permute-start(bf16[4,16,320]{1,0,2:T(4,128)(2,1)S(1)} %all_gather.25), channel_id=1, source_target_pairs={{4,0},{8,4},{12,8},{5,1},{9,5},{13,9},{6,2},{10,6},{14,10},{7,3},{... | collective-permute-start | bytes 122888 | tf_op jit(solution)/shard_map/while/body/eval_jaxpr/ppermute | solution.py:48
  166.5 10.6 %collective-permute-start.2 = (bf16[4,16,320]{1,0,2:T(4,128)(2,1)S(1)}, bf16[4,16,320]{1,0,2:T(4,128)(2,1)S(1)}, u32[]{:S(2)}, u32[]{:S(2)}) collective-permute-start(bf16[4,16,320]{1,0,2:T(4,128)(2,1)S(1)} %all_gather.25), channel_id=1, source_target_pairs={{0,4},{4,8},{8,12},{1,5},{5,9},{9,13},{2,6},{6,10},{10,14},{3,7},{... | collective-permute-start | bytes 122888 | tf_op jit(solution)/shard_map/while/body/eval_jaxpr/ppermute | solution.py:48
  169.9 11.4 %collective-permute-start.3 = (bf16[4,16,320]{1,0,2:T(4,128)(2,1)S(1)}, bf16[4,16,320]{1,0,2:T(4,128)(2,1)S(1)}, u32[]{:S(2)}, u32[]{:S(2)}) collective-permute-start(bf16[4,16,320]{1,0,2:T(4,128)(2,1)S(1)} %all_gather.25), channel_id=1, source_target_pairs={{4,0},{8,4},{12,8},{5,1},{9,5},{13,9},{6,2},{10,6},{14,10},{7,3},{... | collective-permute-start | bytes 122888 | tf_op jit(solution)/shard_map/while/body/eval_jaxpr/ppermute | solution.py:48
  189.5 10.6 %collective-permute-start.2 = (bf16[4,16,320]{1,0,2:T(4,128)(2,1)S(1)}, bf16[4,16,320]{1,0,2:T(4,128)(2,1)S(1)}, u32[]{:S(2)}, u32[]{:S(2)}) collective-permute-start(bf16[4,16,320]{1,0,2:T(4,128)(2,1)S(1)} %all_gather.25), channel_id=1, source_target_pairs={{0,4},{4,8},{8,12},{1,5},{5,9},{9,13},{2,6},{6,10},{10,14},{3,7},{... | collective-permute-start | bytes 122888 | tf_op jit(solution)/shard_map/while/body/eval_jaxpr/ppermute | solution.py:48
  192.8 11.4 %collective-permute-start.3 = (bf16[4,16,320]{1,0,2:T(4,128)(2,1)S(1)}, bf16[4,16,320]{1,0,2:T(4,128)(2,1)S(1)}, u32[]{:S(2)}, u32[]{:S(2)}) collective-permute-start(bf16[4,16,320]{1,0,2:T(4,128)(2,1)S(1)} %all_gather.25), channel_id=1, source_target_pairs={{4,0},{8,4},{12,8},{5,1},{9,5},{13,9},{6,2},{10,6},{14,10},{7,3},{... | collective-permute-start | bytes 122888 | tf_op jit(solution)/shard_map/while/body/eval_jaxpr/ppermute | solution.py:48
  206.1 19.3 %all-reduce.12.cloned.1.call-start = ((), (), s32[]{:S(2)}) async-start(), calls=%async_computation.6 | async-start | bytes 196608 | tf_op jit(solution)/shard_map/while/body/eval_jaxpr/psum | solution.py:170
  236.6 21.1 %all-reduce.12.cloned.1.call-start = ((), (), s32[]{:S(2)}) async-start(), calls=%async_computation.6 | async-start | bytes 196608 | tf_op jit(solution)/shard_map/while/body/eval_jaxpr/psum | solution.py:170
  268.9 21.1 %all-reduce.12.cloned.1.call-start = ((), (), s32[]{:S(2)}) async-start(), calls=%async_computation.6 | async-start | bytes 196608 | tf_op jit(solution)/shard_map/while/body/eval_jaxpr/psum | solution.py:170
  294.6 6.0 collective-permute-start.5
  303.2 9.5 %all-to-all-start.2 = ((bf16[4,2,5120]{2,1,0:T(2,128)(2,1)}), bf16[4,2,5120]{2,1,0:T(2,128)(2,1)S(1)}, u32[]{:S(2)}, u32[]{:S(2)}) async-start(bf16[4,2,5120]{2,1,0:T(2,128)(2,1)} %reshape.198), calls=%async_computation.2 | async-start | bytes 163840 | tf_op jit(solution)/shard_map/all_to_all | solution.py:69
  316.3 9.1 all-to-all-start.3
  326.1 21.1 %all-reduce.14.cloned.1.call-start = ((), (), s32[]{:S(2)}) async-start(), calls=%async_computation.7 | async-start | bytes 196608 | tf_op jit(solution)/shard_map/while/body/eval_jaxpr/psum | solution.py:170
  357.8 20.8 %all-reduce.14.cloned.1.call-start = ((), (), s32[]{:S(2)}) async-start(), calls=%async_computation.7 | async-start | bytes 196608 | tf_op jit(solution)/shard_map/while/body/eval_jaxpr/psum | solution.py:170
  389.2 20.8 %all-reduce.14.cloned.1.call-start = ((), (), s32[]{:S(2)}) async-start(), calls=%async_computation.7 | async-start | bytes 196608 | tf_op jit(solution)/shard_map/while/body/eval_jaxpr/psum | solution.py:170
  430.8 20.0 %collective-permute-start.8 = (f32[1,115200]{1,0:T(1,128)S(1)}, f32[1,115200]{1,0:T(1,128)S(1)}, u32[]{:S(2)}, u32[]{:S(2)}) collective-permute-start(f32[1,115200]{1,0:T(1,128)S(1)} %get-tuple-element.1398), channel_id=1, source_target_pairs={{0,4},{4,0},{8,12},{12,8},{1,5},{5,1},{9,13},{13,9},{2,6},{6,2},{1... | collective-permute-start | bytes 1382408 | tf_op jit(solution)/shard_map/ppermute | solution.py:31
  432.3 34.2 %collective-permute-start.9 = (f32[1,115200]{1,0:T(1,128)S(1)}, f32[1,115200]{1,0:T(1,128)S(1)}, u32[]{:S(2)}, u32[]{:S(2)}) collective-permute-start(f32[1,115200]{1,0:T(1,128)S(1)} %get-tuple-element.1397), channel_id=1, source_target_pairs={{0,8},{4,12},{8,0},{12,4},{1,9},{5,13},{9,1},{13,5},{2,10},{6,14},... | collective-permute-start | bytes 1382408 | tf_op jit(solution)/shard_map/ppermute | solution.py:31
  433.3 33.2 %collective-permute-start.10 = (f32[1,115200]{1,0:T(1,128)S(1)}, f32[1,115200]{1,0:T(1,128)S(1)}, u32[]{:S(2)}, u32[]{:S(2)}) collective-permute-start(f32[1,115200]{1,0:T(1,128)S(1)} %get-tuple-element.1396), channel_id=1, source_target_pairs={{0,12},{4,8},{8,4},{12,0},{1,13},{5,9},{9,5},{13,1},{2,14},{6,10},... | collective-permute-start | bytes 1382408 | tf_op jit(solution)/shard_map/ppermute | solution.py:31
  789.5 51.8 %all-to-all-start.4 = ((f32[4,1,115200]{2,1,0:T(1,128)}), f32[4,1,115200]{2,1,0:T(1,128)}, u32[]{:S(2)}, u32[]{:S(2)}) async-start(f32[4,1,115200]{2,1,0:T(1,128)} %copy.59), calls=%async_computation.4 | async-start | bytes 3686400 | tf_op jit(solution)/shard_map/all_to_all | solution.py:77
  799.9 101.3 %all-reduce.10.cloned.1.call-start = ((), (), s32[]{:S(2)}) async-start(), calls=%async_computation.5 | async-start | bytes 3686400 | tf_op jit(solution)/shard_map/psum | solution.py:250
  (51 other events, 495.5 us)
Sparse Core Ops, SparseCore 0:
  209.3 16.0 all-reduce.11
  239.9 17.7 all-reduce.11
  272.1 17.7 all-reduce.11
  329.0 18.1 all-reduce.13
  360.8 17.7 all-reduce.13
  392.1 17.7 all-reduce.13
Sparse Core Ops, SparseCore 1:
  844.9 56.1 all-reduce.9
